TPU v7x, 32 devices: a whole 2x2x4 slice. The times are simulated.
32 devices in a mesh: dp: 8 (over z, core), mp: 4 (over y, x).
Axes of the slice: x: 2, y: 2, z: 4, core: 2. Of those that a mesh axis runs over, the one named last changes fastest.
Arguments:
- tokens: bfloat16 [16384, 1280], P(('dp', 'mp')), may hold values from -6 to 6
- cotangent: bfloat16 [16384, 1280], P(('dp', 'mp')), may hold values from -6 to 6
- lengths: int32 [16], replicated, may hold values from 256 to 1024, as said below
- dealing: int32 [16], replicated, may hold values from 0 to 15, as said below
- gain_one: bfloat16 [1280], P('mp'), may hold values from 0.5 to 1.5
- gain_two: bfloat16 [1280], P('mp'), may hold values from 0.5 to 1.5
- attention_in: bfloat16 [1280, 3, 1280], P('mp'), may hold values from -0.15625 to 0.15625
- query_scale: float32 [80], replicated, may hold values from 0 to 1.5
- attention_out: bfloat16 [1280, 1280], P('mp'), may hold values from -1.25 to 1.25
- hidden_in: bfloat16 [1280, 1280], P('mp'), may hold values from -0.15625 to 0.15625
- hidden_out: bfloat16 [1280, 1280], P('mp'), may hold values from -0.3125 to 0.3125
Outputs:
- layer_out: bfloat16 [16384, 1280], P(('dp', 'mp'))
- tokens_grad: float32 [16384, 1280], P(('dp', 'mp'))
- series_cache: bfloat16 [2, 16384, 1280], P(None, 'dp', 'mp')
- gain_one_grad: float32 [1280], P('mp')
- gain_two_grad: float32 [1280], P('mp')
- attention_in_grad: float32 [1280, 3, 1280], P('mp')
- query_scale_grad: float32 [80], replicated
- attention_out_grad: float32 [1280, 1280], P('mp')
- hidden_in_grad: float32 [1280, 1280], P('mp')
- hidden_out_grad: float32 [1280, 1280], P('mp')
Inputs may be any that keep to these rules, and one draw needn't show every extreme that they name: `lengths`: series s belongs to group s // 2; every group has a series of exactly 1024 tokens. A permutation of the 16 places: series s goes to group dealing[s] // 2 at place dealing[s] % 2. The series of one group go to one group at most 1 at a time, and in every draw some group sends exactly 1 series to some group.
All inputs are finite; a program needn't handle non-finite values.
Results may differ from a plain program's by a relative error of at most 0.02.
Values may be sent and summed in bfloat16 or wider, within the bound.
No kernel may reach another device: no remote copies, remote signals or barrier semaphores. Data moves between devices by JAX's collectives and lax.ppermute only.
A program may use at most 256 MiB of HBM per device.

v0:
```python
import math

import jax
import jax.numpy as jnp
from jax import lax
from jax.experimental import pallas as pl
from jax.experimental.pallas import tpu as pltpu
from jax.sharding import PartitionSpec as P


D = 1280
NH = 16
HD = 80
LMAX = 1024
BLK = 128
TQ = 128


epsilon = 1e-06
scale_base = 1.442695041
masked_score = -1e30


def lookup(values_table, positions):
    entries = jnp.arange(values_table.shape[0], dtype=jnp.int32)
    picked = jnp.where(positions[:, None] == entries[None, :], values_table[None, :], 0)
    return jnp.sum(picked, axis=1)


def packing(span_len, group_rows):
    blocks = (span_len + BLK - 1) // BLK
    block_ends = BLK * jnp.cumsum(blocks)
    starts = block_ends - BLK * blocks
    in_group = jnp.arange(group_rows, dtype=jnp.int32)
    series_at = jnp.sum((block_ends[None, :] <= in_group[:, None]).astype(jnp.int32), axis=1)
    capped = jnp.minimum(series_at, span_len.shape[0] - 1)
    offset = in_group - lookup(starts, capped)
    live_row = (series_at < span_len.shape[0]) & (offset < lookup(span_len, capped))
    return (starts, series_at, capped, offset, live_row)


def slot_table(slot_of, starts, span_len, slot_count):
    entries = jnp.arange(slot_count, dtype=jnp.int32)
    matched = slot_of[None, :] == entries[:, None]
    slot_first = jnp.sum(jnp.where(matched, starts[None, :], 0), axis=1)
    slot_length = jnp.sum(jnp.where(matched, span_len[None, :], 0), axis=1)
    return (slot_first, slot_length)


def series_maps(lengths, dealing, series_grp, group_rows, my_group):
    groups = lengths.shape[0] // series_grp
    capacity = (series_grp + groups - 1) // groups
    places = jnp.arange(series_grp, dtype=jnp.int32)
    target = dealing.reshape(groups, series_grp) // series_grp
    earlier = (target[:, :, None] == target[:, None, :]) & (
        places[None, None, :] < places[None, :, None]
    )
    rank_of = jnp.sum(earlier.astype(jnp.int32), axis=2)
    slot_of = (target * capacity + rank_of).reshape(-1)
    rank_flat = rank_of.reshape(-1)
    src_len = lax.dynamic_slice_in_dim(lengths, my_group * series_grp, series_grp)
    src_slot = lax.dynamic_slice_in_dim(slot_of, my_group * series_grp, series_grp)
    src_starts, _, src_capped, src_offset, src_live = packing(src_len, group_rows)
    dealt_places = jnp.arange(lengths.shape[0], dtype=jnp.int32)
    owner = jnp.sum(
        jnp.where(dealing[None, :] == dealt_places[:, None], dealt_places[None, :], 0), axis=1
    )
    my_series = lax.dynamic_slice_in_dim(owner, my_group * series_grp, series_grp)
    dst_len = lookup(lengths, my_series)
    dst_slot = my_series // series_grp * capacity + lookup(rank_flat, my_series)
    dst_starts, dst_at, dst_capped, dst_offset, dst_live = packing(dst_len, group_rows)
    slot_count = groups * capacity
    send_first, send_len = slot_table(src_slot, src_starts, src_len, slot_count)
    back_first, back_len = slot_table(dst_slot, dst_starts, dst_len, slot_count)
    src_index = lookup(src_slot, src_capped) * LMAX + src_offset
    dst_index = lookup(dst_slot, dst_capped) * LMAX + dst_offset
    key_live = jnp.where(dst_at < series_grp, dst_live, True)
    return (
        send_first,
        send_len,
        back_first,
        back_len,
        src_index,
        src_live,
        dst_index,
        dst_live,
        dst_at,
        key_live,
    )


def send_windows(values, slot_first, slot_length, my_group, groups):
    padded = jnp.pad(values, ((0, 0), (0, LMAX), (0, 0)))
    positions = jnp.arange(LMAX, dtype=jnp.int32)[None, :, None]
    windows = []
    for shift in range(groups):
        target = (my_group + shift) % groups
        window = lax.dynamic_slice_in_dim(padded, slot_first[target], LMAX, axis=1)
        windows.append(
            jnp.where(positions < slot_length[target], window, jnp.zeros((), values.dtype))
        )
    return windows


def place_slots(stacked, place_shift, place_start, place_len, out_rows):
    rows = jnp.arange(out_rows, dtype=jnp.int32)[None, :, None]
    placed = jnp.zeros((stacked.shape[1], out_rows, stacked.shape[3]), stacked.dtype)
    for q in range(place_shift.shape[0]):
        window = lax.dynamic_index_in_dim(stacked, place_shift[q], axis=0, keepdims=False)
        padded = jnp.pad(window, ((0, 0), (out_rows, out_rows - LMAX), (0, 0)))
        shifted = lax.dynamic_slice_in_dim(padded, out_rows - place_start[q], out_rows, axis=1)
        inside = (rows >= place_start[q]) & (rows < place_start[q] + place_len[q])
        placed = jnp.where(inside, shifted, placed)
    return placed


def dealt_places(lengths, dealing, series_grp, my_group):
    dealt_places = jnp.arange(lengths.shape[0], dtype=jnp.int32)
    owner = jnp.sum(
        jnp.where(dealing[None, :] == dealt_places[:, None], dealt_places[None, :], 0), axis=1
    )
    my_series = lax.dynamic_slice_in_dim(owner, my_group * series_grp, series_grp)
    place_len = lookup(lengths, my_series)
    blocks = (place_len + BLK - 1) // BLK
    place_start = BLK * jnp.cumsum(blocks) - BLK * blocks
    return my_series // series_grp, place_start, place_len


def block_bounds(src_len, group_rows):
    starts, series_at, _, _, live_row = packing(src_len, group_rows)
    first_rows = jnp.arange(group_rows // TQ, dtype=jnp.int32) * TQ
    seg = series_at[first_rows]
    inside = seg < src_len.shape[0]
    seg_c = jnp.minimum(seg, src_len.shape[0] - 1)
    block_start = jnp.where(inside, lookup(starts, seg_c), 0)
    block_end = jnp.where(inside, block_start + lookup(src_len, seg_c), 0)
    return block_start.astype(jnp.int32), block_end.astype(jnp.int32), live_row


def _window(i, rows, width):
    qs = i * TQ
    ws = jnp.minimum(jnp.maximum(qs - (width - TQ), 0), rows - width)
    return qs, pl.multiple_of(ws, TQ)


def _allowed(qs, ws, s0, e0, width):
    a = qs + lax.broadcasted_iota(jnp.int32, (TQ, width), 0)
    b = ws + lax.broadcasted_iota(jnp.int32, (TQ, width), 1)
    return (b >= s0) & (b <= a) & (b < e0)


def _fwd_block(i, s0, e0, q_ref, k_ref, v_ref, o_ref, lse_ref, width):
    heads, rows = k_ref.shape[0], k_ref.shape[1]
    qs, ws = _window(i, rows, width)
    allowed = _allowed(qs, ws, s0, e0, width)
    for h in range(heads):
        q = q_ref[h]
        k = k_ref[h, pl.ds(ws, width), :]
        v = v_ref[h, pl.ds(ws, width), :]
        s = lax.dot_general(q, k, (((1,), (1,)), ((), ())), preferred_element_type=jnp.float32)
        s = jnp.where(allowed, s, masked_score)
        m = jnp.max(s, axis=1, keepdims=True)
        p = jnp.exp(s - m)
        l = jnp.sum(p, axis=1, keepdims=True)
        probs = (p / l).astype(jnp.bfloat16)
        o = jnp.dot(probs, v, preferred_element_type=jnp.float32)
        o_ref[h] = o.astype(o_ref.dtype)
        lse_ref[h] = m + jnp.log(l)


def attn_fwd_kernel(starts_ref, ends_ref, q_ref, k_ref, v_ref, o_ref, lse_ref):
    i = pl.program_id(0)
    s0 = starts_ref[i]
    e0 = ends_ref[i]
    short = i * TQ + TQ - s0 <= LMAX // 2

    @pl.when((s0 < e0) & short)
    def _():
        _fwd_block(i, s0, e0, q_ref, k_ref, v_ref, o_ref, lse_ref, LMAX // 2)

    @pl.when((s0 < e0) & jnp.logical_not(short))
    def _():
        _fwd_block(i, s0, e0, q_ref, k_ref, v_ref, o_ref, lse_ref, LMAX)

    @pl.when(s0 >= e0)
    def _():
        o_ref[...] = jnp.zeros(o_ref.shape, o_ref.dtype)
        lse_ref[...] = jnp.zeros(lse_ref.shape, lse_ref.dtype)


def _bwd_block(i, s0, e0, q_ref, k_ref, v_ref, do_ref, lse_ref, dq_ref, dk_acc, dv_acc, width):
    heads, rows = k_ref.shape[0], k_ref.shape[1]
    qs, ws = _window(i, rows, width)
    allowed = _allowed(qs, ws, s0, e0, width)
    for h in range(heads):
        q = q_ref[h]
        k = k_ref[h, pl.ds(ws, width), :]
        v = v_ref[h, pl.ds(ws, width), :]
        do = do_ref[h]
        s = lax.dot_general(q, k, (((1,), (1,)), ((), ())), preferred_element_type=jnp.float32)
        s = jnp.where(allowed, s, masked_score)
        probs = jnp.exp(s - lse_ref[h])
        dp = lax.dot_general(do, v, (((1,), (1,)), ((), ())), preferred_element_type=jnp.float32)
        row_dot = jnp.sum(probs * dp, axis=1, keepdims=True)
        ds = (probs * (dp - row_dot)).astype(jnp.bfloat16)
        dq = jnp.dot(ds, k, preferred_element_type=jnp.float32)
        dq_ref[h] = dq.astype(dq_ref.dtype)
        dk_acc[h, pl.ds(ws, width), :] += jnp.dot(ds.T, q, preferred_element_type=jnp.float32)
        dv_acc[h, pl.ds(ws, width), :] += jnp.dot(
            probs.astype(jnp.bfloat16).T, do, preferred_element_type=jnp.float32
        )


def attn_bwd_kernel(starts_ref, ends_ref, q_ref, k_ref, v_ref, do_ref, lse_ref,
                    dq_ref, dk_ref, dv_ref, dk_acc, dv_acc):
    i = pl.program_id(0)
    s0 = starts_ref[i]
    e0 = ends_ref[i]
    short = i * TQ + TQ - s0 <= LMAX // 2

    @pl.when(i == 0)
    def _():
        dk_acc[...] = jnp.zeros(dk_acc.shape, dk_acc.dtype)
        dv_acc[...] = jnp.zeros(dv_acc.shape, dv_acc.dtype)

    @pl.when((s0 < e0) & short)
    def _():
        _bwd_block(i, s0, e0, q_ref, k_ref, v_ref, do_ref, lse_ref, dq_ref, dk_acc, dv_acc, LMAX // 2)

    @pl.when((s0 < e0) & jnp.logical_not(short))
    def _():
        _bwd_block(i, s0, e0, q_ref, k_ref, v_ref, do_ref, lse_ref, dq_ref, dk_acc, dv_acc, LMAX)

    @pl.when(s0 >= e0)
    def _():
        dq_ref[...] = jnp.zeros(dq_ref.shape, dq_ref.dtype)

    @pl.when(i == pl.num_programs(0) - 1)
    def _():
        dk_ref[...] = dk_acc[...].astype(dk_ref.dtype)
        dv_ref[...] = dv_acc[...].astype(dv_ref.dtype)


def attention_forward(q, k, v, starts, ends):
    heads, rows, width = q.shape
    blocks = rows // TQ
    whole = pl.BlockSpec((heads, rows, width), lambda i, s, e: (0, 0, 0))
    part = pl.BlockSpec((heads, TQ, width), lambda i, s, e: (0, i, 0))
    flops = 4 * heads * rows * LMAX * width
    return pl.pallas_call(
        attn_fwd_kernel,
        grid_spec=pltpu.PrefetchScalarGridSpec(
            num_scalar_prefetch=2,
            grid=(blocks,),
            in_specs=[part, whole, whole],
            out_specs=[part, pl.BlockSpec((heads, TQ, 1), lambda i, s, e: (0, i, 0))],
        ),
        out_shape=[
            jax.ShapeDtypeStruct((heads, rows, width), jnp.bfloat16),
            jax.ShapeDtypeStruct((heads, rows, 1), jnp.float32),
        ],
        compiler_params=pltpu.CompilerParams(
            dimension_semantics=("arbitrary",), vmem_limit_bytes=48 * 1024 * 1024
        ),
        cost_estimate=pl.CostEstimate(
            flops=flops, transcendentals=heads * rows * LMAX, bytes_accessed=4 * q.size * 2
        ),
    )(starts, ends, q, k, v)


def attention_backward(q, k, v, do, lse, starts, ends):
    heads, rows, width = q.shape
    blocks = rows // TQ
    whole = pl.BlockSpec((heads, rows, width), lambda i, s, e: (0, 0, 0))
    part = pl.BlockSpec((heads, TQ, width), lambda i, s, e: (0, i, 0))
    flops = 10 * heads * rows * LMAX * width
    return pl.pallas_call(
        attn_bwd_kernel,
        grid_spec=pltpu.PrefetchScalarGridSpec(
            num_scalar_prefetch=2,
            grid=(blocks,),
            in_specs=[part, whole, whole, part, pl.BlockSpec((heads, TQ, 1), lambda i, s, e: (0, i, 0))],
            out_specs=[part, whole, whole],
            scratch_shapes=[
                pltpu.VMEM((heads, rows, width), jnp.float32),
                pltpu.VMEM((heads, rows, width), jnp.float32),
            ],
        ),
        out_shape=[jax.ShapeDtypeStruct((heads, rows, width), jnp.bfloat16)] * 3,
        compiler_params=pltpu.CompilerParams(
            dimension_semantics=("arbitrary",), vmem_limit_bytes=48 * 1024 * 1024
        ),
        cost_estimate=pl.CostEstimate(
            flops=flops, transcendentals=heads * rows * LMAX, bytes_accessed=7 * q.size * 2
        ),
    )(starts, ends, q, k, v, do, lse)


def per_device(
    tokens,
    cotangent,
    lengths,
    dealing,
    gain_one,
    gain_two,
    attention_in,
    query_scale,
    attention_out,
    hidden_in,
    hidden_out,
):
    out_all, in_all, down_all = (
        lax.all_gather(attention_out, "mp", axis=0, tiled=True),
        lax.all_gather(hidden_in, "mp", axis=0, tiled=True),
        lax.all_gather(hidden_out, "mp", axis=0, tiled=True),
    )
    row_count = tokens.shape[0]
    mp_count = lax.axis_size("mp")
    my_group = lax.axis_index("dp")
    my_part = lax.axis_index("mp")
    group_rows = row_count * mp_count
    series_grp = group_rows // LMAX
    heads_here = NH // mp_count
    width_here = heads_here * HD
    shard_width = D // mp_count
    maps = series_maps(lengths, dealing, series_grp, group_rows, my_group)
    send_first, send_len = maps[0], maps[1]
    place_slot, place_start, place_len = dealt_places(lengths, dealing, series_grp, my_group)
    src_len = lax.dynamic_slice_in_dim(lengths, my_group * series_grp, series_grp)
    block_start, block_end, src_live = block_bounds(src_len, group_rows)
    live_mine = lax.dynamic_slice_in_dim(src_live, my_part * row_count, row_count).astype(
        jnp.float32
    )[:, None]
    gain_rows = jnp.zeros((8, D), jnp.bfloat16)
    gain_rows = gain_rows.at[0, :shard_width].set(gain_one).at[0, shard_width : 2 * shard_width].set(gain_two)
    packed = lax.all_gather(jnp.concatenate([tokens, gain_rows]), "mp", axis=0, tiled=False)
    gain_first = packed[:, row_count, :shard_width].reshape(D).astype(jnp.float32)
    gain_second = packed[:, row_count, shard_width : 2 * shard_width].reshape(D).astype(jnp.float32)
    inputs_group = packed[:, :row_count].reshape(group_rows, D).astype(jnp.float32)
    inv_group = lax.rsqrt(jnp.mean(inputs_group * inputs_group, axis=1, keepdims=True) + epsilon)
    normed_group = (inputs_group * inv_group * gain_first).astype(jnp.bfloat16)
    inputs = tokens.astype(jnp.float32)
    inv_one = lax.rsqrt(jnp.mean(inputs * inputs, axis=1, keepdims=True) + epsilon)
    weight_heads = attention_in.reshape(heads_here, HD, 3, D)
    projected = jnp.einsum(
        "rd,hecd->chre", normed_group, weight_heads, preferred_element_type=jnp.float32
    )
    dim_scale = scale_base / math.sqrt(HD) * jax.nn.softplus(query_scale)
    query_raw = projected[0]
    queries = (query_raw * dim_scale).astype(jnp.bfloat16)
    keys = projected[1].astype(jnp.bfloat16)
    values = projected[2].astype(jnp.bfloat16)
    kv_rows = jnp.stack([keys, values]).transpose(0, 2, 1, 3).reshape(2, group_rows, width_here)
    groups = lax.axis_size("dp")
    windows = send_windows(kv_rows, send_first, send_len, my_group, groups)
    received = [windows[0]] + [
        lax.ppermute(
            windows[shift], "dp", [(r, (r + shift) % groups) for r in range(groups)]
        )
        for shift in range(1, groups)
    ]
    place_shift = (my_group - place_slot) % groups
    received = jnp.stack(received)
    mixed, log_total = attention_forward(queries, keys, values, block_start, block_end)
    att_group = jnp.where(src_live[None, :, None], mixed, jnp.zeros((), jnp.bfloat16))
    att_heads = lax.all_to_all(att_group, "mp", split_axis=1, concat_axis=0, tiled=True)
    out_heads = out_all.reshape(NH, HD, D)
    branch = jnp.einsum("hie,hed->id", att_heads, out_heads, preferred_element_type=jnp.float32)
    first_sum = inputs + branch
    inv_two = lax.rsqrt(jnp.mean(first_sum * first_sum, axis=1, keepdims=True) + epsilon)
    normed_two = (first_sum * inv_two * gain_second).astype(jnp.bfloat16)
    preact = jnp.einsum("rd,fd->rf", normed_two, in_all, preferred_element_type=jnp.float32)
    hidden = jax.nn.silu(preact).astype(jnp.bfloat16)
    feed = jnp.dot(hidden, down_all, preferred_element_type=jnp.float32)
    layer_out = ((first_sum + feed) * live_mine).astype(jnp.bfloat16)
    out_grad = cotangent.astype(jnp.float32) * live_mine
    feed_grad = out_grad.astype(jnp.bfloat16)
    hidden_grad = jnp.einsum("rd,fd->rf", feed_grad, down_all, preferred_element_type=jnp.float32)
    gate_sig = jax.nn.sigmoid(preact)
    preact_grad = (hidden_grad * gate_sig * (1.0 + preact * (1.0 - gate_sig))).astype(jnp.bfloat16)
    normed_two_grad = jnp.dot(preact_grad, in_all, preferred_element_type=jnp.float32)
    scaled_two = gain_second * normed_two_grad
    first_grad = (
        out_grad
        + inv_two * scaled_two
        - first_sum * inv_two**3 * jnp.mean(scaled_two * first_sum, axis=1, keepdims=True)
    )
    branch_grad = first_grad.astype(jnp.bfloat16)
    att_heads_grad = jnp.einsum(
        "id,hed->hie", branch_grad, out_heads, preferred_element_type=jnp.float32
    ).astype(jnp.bfloat16)
    grad_group = lax.all_to_all(att_heads_grad, "mp", split_axis=0, concat_axis=1, tiled=True)
    grad_heads = jnp.where(src_live[None, :, None], grad_group, jnp.zeros((), jnp.bfloat16))
    out_part = jnp.einsum(
        "hie,id->hed", att_heads, branch_grad, preferred_element_type=jnp.float32
    ).reshape(D, D)
    in_part = jnp.einsum("ru,rd->ud", preact_grad, normed_two, preferred_element_type=jnp.float32)
    down_part = jnp.einsum("ru,rd->ud", hidden, feed_grad, preferred_element_type=jnp.float32)
    row_terms = jnp.stack([out_part, in_part, down_part], axis=1)
    shares = lax.psum_scatter(
        row_terms.astype(jnp.bfloat16), "mp", scatter_dimension=0, tiled=True
    )
    query_scaled_grad, key_grad, value_grad = attention_backward(
        queries, keys, values, grad_heads, log_total, block_start, block_end
    )
    live_heads = src_live[None, :, None]
    query_scaled_grad = jnp.where(live_heads, query_scaled_grad, jnp.zeros((), jnp.bfloat16)).astype(
        jnp.float32
    )
    query_grad = (query_scaled_grad * dim_scale).astype(jnp.bfloat16)
    proj_grad = jnp.stack(
        [
            query_grad,
            jnp.where(live_heads, key_grad, jnp.zeros((), jnp.bfloat16)),
            jnp.where(live_heads, value_grad, jnp.zeros((), jnp.bfloat16)),
        ]
    )
    qkv_part = jnp.einsum(
        "chre,rd->hecd", proj_grad, normed_group, preferred_element_type=jnp.float32
    ).reshape(width_here, 3, D)
    normed_one_part = jnp.einsum(
        "chre,hecd->rd", proj_grad, weight_heads, preferred_element_type=jnp.float32
    )
    normed_one_part, qkv_part, shares, query_raw = lax.optimization_barrier(
        (normed_one_part, qkv_part, shares, query_raw)
    )
    cache = place_slots(received, place_shift, place_start, place_len, group_rows)
    scale_part = (
        jnp.sum(query_scaled_grad * query_raw, axis=(0, 1))
        * (scale_base / math.sqrt(HD))
        * jax.nn.sigmoid(query_scale)
    )
    normed_one_grad = lax.psum_scatter(
        normed_one_part.astype(jnp.bfloat16), "mp", scatter_dimension=0, tiled=True
    ).astype(jnp.float32)
    scaled_one = gain_first * normed_one_grad
    tokens_grad = (
        first_grad
        + inv_one * scaled_one
        - inputs * inv_one**3 * jnp.mean(scaled_one * inputs, axis=1, keepdims=True)
    )
    gain_one_part = jnp.sum(normed_one_part * inputs_group * inv_group, axis=0)
    gain_two_part = jnp.sum(normed_two_grad * first_sum * inv_two, axis=0)
    small = jnp.concatenate(
        [
            gain_one_part.reshape(mp_count, shard_width),
            gain_two_part.reshape(mp_count, shard_width),
            jnp.broadcast_to(scale_part, (mp_count, HD)),
        ],
        axis=1,
    )
    small = lax.psum(lax.psum_scatter(small, "mp", scatter_dimension=0, tiled=True), "dp")
    gain_one_grad = small[0, :shard_width]
    gain_two_grad = small[0, shard_width : 2 * shard_width]
    query_scale_grad = small[0, 2 * shard_width :]
    totals = lax.psum(
        jnp.concatenate([qkv_part.astype(jnp.bfloat16), shares], axis=1), "dp"
    ).astype(jnp.float32)
    return (
        layer_out,
        tokens_grad,
        cache,
        gain_one_grad,
        gain_two_grad,
        totals[:, 0:3],
        query_scale_grad,
        totals[:, 3],
        totals[:, 4],
        totals[:, 5],
    )


def solution(mesh):
    placed = (
        P(("dp", "mp"), None),
        P(("dp", "mp"), None),
        P(),
        P(),
        P("mp"),
        P("mp"),
        P("mp", None, None),
        P(),
        P("mp", None),
        P("mp", None),
        P("mp", None),
    )
    return jax.shard_map(
        per_device,
        mesh=mesh,
        in_specs=placed,
        out_specs=(
            P(("dp", "mp"), None),
            P(("dp", "mp"), None),
            P(None, "dp", "mp"),
            P("mp"),
            P("mp"),
            P("mp", None, None),
            P(),
            P("mp", None),
            P("mp", None),
            P("mp", None),
        ),
        check_vma=False,
    )
```

profile of v0, /device:TPU:0, one launch (start us, length us, event | category | flops | bytes accessed | tf_op | source)
XLA Modules:
  0.0 779.3 jit_solution(14096409073305738366)
XLA Ops:
  21.0 60.8 %all-gather.12.cloned.1.call-done = bf16[2080,1280]{1,0:T(8,128)(2,1)} async-done(((bf16[520,1280]{1,0:T(8,128)(2,1)}), bf16[2080,1280]{1,0:T(8,128)(2,1)}) %all-gather.12.cloned.1.call-update) | async-done | bytes 5324816 | tf_op jit(solution)/shard_map/all_gather | solution.py:336
  90.1 8.4 %convolution_bitcast_fusion.1 = f32[3,4,2048,80]{3,2,1,0:T(8,128)S(1)} fusion(bf16[2048,1280,1,1]{1,0,2,3:T(8,128)(2,1)S(1)} %bitcast.178, bf16[4,80,3,1280]{3,1,0,2:T(8,128)(2,1)S(1)} %bitcast.162), kind=kOutput, calls=%fused_computation.21 | convolution fusion | flops 5033164800 | bytes 15564800 | tf_op jit(solution)/shard_map/rd,hecd->chre/dot_general | solution.py:345
  103.5 6.9 fusion.60
  110.4 27.6 %shard_map.186 = (bf16[4,2048,80]{2,1,0:T(8,128)(2,1)S(1)}, f32[4,2048,1]{2,1,0:T(8,128)}) custom-call(s32[16]{0:T(128)S(1)} %get-tuple-element.94.starts_ref, s32[16]{0:T(128)S(1)} %get-tuple-element.93.ends_ref, bf16[4,2048,80]{2,1,0:T(8,128)(2,1)S(1)} %multiply_convert_fusion.q_ref, bf16[4,2048,80]{2,1,0:T(8,128)(2,1)} %bitcast.174, ...), custom_call_target="tpu_custom_call" | custom-call | flops 2684354560 | bytes 5242880 | tf_op jit(solution)/shard_map/pallas_call | solution.py:250
  138.4 10.7 %copy.44 = bf16[4,2048,80]{2,0,1:T(4,128)(2,1)} copy(bf16[4,2048,80]{2,1,0:T(8,128)(2,1)S(1)} %broadcast_select_fusion.1) | data formatting | bytes 2621440 | tf_op jit(solution)/shard_map/jit(_where)/select_n | solution.py:365
  153.8 39.5 %all-to-all-done = bf16[4,2048,80]{2,0,1:T(4,128)(2,1)} async-done(((bf16[4,2048,80]{2,0,1:T(4,128)(2,1)}), bf16[4,2048,80]{2,0,1:T(4,128)(2,1)}, u32[]{:S(2)}, u32[]{:S(2)}) %all-to-all-start) | async-done | bytes 1310752 | tf_op jit(solution)/shard_map/all_to_all | solution.py:366
  197.8 6.2 multiply_reduce_fusion.2
  214.4 27.4 %all-gather.10.cloned.1.call-done = bf16[1280,1280]{1,0:T(8,128)(2,1)} async-done(((bf16[320,1280]{1,0:T(8,128)(2,1)}), bf16[1280,1280]{1,0:T(8,128)(2,1)}) %all-gather.10.cloned.1.call-update) | async-done | bytes 3276816 | tf_op jit(solution)/shard_map/all_gather | solution.py:315
  259.8 5.7 fusion.26
  269.8 6.0 fusion.4
  280.3 21.0 %all-to-all-done.1 = bf16[16,512,80]{1,2,0:T(8,128)(2,1)} async-done(((bf16[16,512,80]{1,2,0:T(8,128)(2,1)}), bf16[16,512,80]{1,2,0:T(8,128)(2,1)}, u32[]{:S(2)}, u32[]{:S(2)}) %all-to-all-start.1) | async-done | bytes 1310752 | tf_op jit(solution)/shard_map/all_to_all | solution.py:392
  308.1 34.9 %shard_map.187 = (bf16[4,2048,80]{2,1,0:T(8,128)(2,1)S(1)}, bf16[4,2048,80]{2,1,0:T(8,128)(2,1)S(1)}, bf16[4,2048,80]{2,1,0:T(8,128)(2,1)}) custom-call(s32[16]{0:T(128)S(1)} %get-tuple-element.94.starts_ref, s32[16]{0:T(128)S(1)} %get-tuple-element.93.ends_ref, bf16[4,2048,80]{2,1,0:T(8,128)(2,1)} %copy-done.4, bf16[4,2048,80]{2,1,0:T(8,128)(2,1)} %bitcast.175, ...), custom_call_target="tpu_custom_call" | custom-call | flops 6710886400 | bytes 9175040 | tf_op jit(solution)/shard_map/pallas_call | solution.py:277
  345.9 9.7 %convolution_bitcast_fusion = f32[2048,1280]{1,0:T(8,128)} fusion(bf16[4,80,3,1280]{3,1,0,2:T(8,128)(2,1)S(1)} %bitcast.163, bf16[1,4,2048,80]{3,2,1,0:T(8,128)(2,1)S(1)} %get-tuple-element.90, bf16[1,4,2048,80]{3,2,1,0:T(8,128)(2,1)S(1)} %get-tuple-element.89, bf16[1,4,2048,80]{3,2,1,0:T(8,128)(2,1)S(1)} %fusion.25), kind=kOutput, calls=%fused_computation.13 | convolution fusion | flops 5037096960 | bytes 16875520 | tf_op jit(solution)/shard_map/chre,hecd->rd/dot_general | solution.py:421
  355.6 6.4 fusion.10
  362.0 10.1 %reduce-scatter.3.cloned.1.call-done = bf16[320,3,1280]{2,0,1:T(8,128)(2,1)} async-done(((bf16[1280,3,1280]{2,0,1:T(8,128)(2,1)}), bf16[320,3,1280]{2,0,1:T(8,128)(2,1)}) %reduce-scatter.3.cloned.1.call-update) | async-done | bytes 2457616 | tf_op jit(solution)/shard_map/reduce_scatter | solution.py:400
  376.5 13.2 %fusion.6 = (f32[1280]{0:T(1024)S(1)}, bf16[2048,1280]{1,0:T(8,128)(2,1)}) fusion(f32[2048,1280]{1,0:T(8,128)} %convolution_bitcast_fusion, f32[2048]{0:T(1024)S(1)} %bitcast.183, bf16[4,520,1280]{2,1,0:T(8,128)(2,1)} %bitcast.168), kind=kLoop, calls=%fused_computation.11 | loop fusion | flops 13105920 | bytes 20984832 | tf_op jit(solution)/shard_map/reduce_sum | solution.py:442
  430.7 6.0 copy.52
  436.7 8.7 %fusion.36 = (bf16[2,1024,320]{1,2,0:T(8,128)(2,1)S(1)}, bf16[2,1024,320]{1,2,0:T(8,128)(2,1)}, bf16[2,1024,320]{1,2,0:T(8,128)(2,1)}, bf16[2,1024,320]{1,2,0:T(...) fusion(s32[]{:T(128)S(6)} %select_n.308, bf16[2,2048,320]{1,2,0:T(8,128)(2,1)} %bitcast.169, ...), kind=kLoop, calls=%fused_computation.92 | loop fusion | flops 3932160 | bytes 10491928 | tf_op jit(solution)/shard_map/jit(_where)/select_n | solution.py:100
  459.3 47.3 %collective-permute-done = bf16[2,1024,320]{1,2,0:T(8,128)(2,1)} collective-permute-done((bf16[2,1024,320]{1,2,0:T(8,128)(2,1)}, bf16[2,1024,320]{1,2,0:T(8,128)(2,1)}, u32[]{:S(2)}, u32[]{:S(2)}) %collective-permute-start) | collective-permute-done | bytes 1310752 | tf_op jit(solution)/shard_map/ppermute | solution.py:357
  509.2 34.5 %collective-permute-start.6 = (bf16[2,1024,320]{1,2,0:T(8,128)(2,1)S(1)}, bf16[2,1024,320]{1,2,0:T(8,128)(2,1)S(1)}, u32[]{:S(2)}, u32[]{:S(2)}) collective-permute-start(bf16[2,1024,320]{1,2,0:T(8,128)(2,1)S(1)} %get-tuple-element.79), channel_id=1, source_target_pairs={{0,28},{4,0},{8,4},{12,8},{16,12},{20,16},{24,20},{28,24},{1,29},{... | collective-permute-start | bytes 3932168 | tf_op jit(solution)/shard_map/ppermute | solution.py:357
  546.1 73.1 %collective-permute-done.2 = bf16[2,1024,320]{1,2,0:T(8,128)(2,1)} collective-permute-done((bf16[2,1024,320]{1,2,0:T(8,128)(2,1)}, bf16[2,1024,320]{1,2,0:T(8,128)(2,1)}, u32[]{:S(2)}, u32[]{:S(2)}) %collective-permute-start.2) | collective-permute-done | bytes 1310752 | tf_op jit(solution)/shard_map/ppermute | solution.py:357
  627.9 24.8 %collective-permute-done.6 = bf16[2,1024,320]{1,2,0:T(8,128)(2,1)S(1)} collective-permute-done((bf16[2,1024,320]{1,2,0:T(8,128)(2,1)S(1)}, bf16[2,1024,320]{1,2,0:T(8,128)(2,1)S(1)}, u32[]{:S(2)}, u32[]{:S(2)}) %collective-permute-start.6) | collective-permute-done | bytes 1310752 | tf_op jit(solution)/shard_map/ppermute | solution.py:357
  663.3 16.1 %all-reduce.4 = f32[4,720]{1,0:T(4,128)S(1)} all-reduce(f32[4,720]{1,0:T(4,128)S(1)} %maximum_maximum_fusion), channel_id=5, replica_groups=mesh['dp'=8,'mp'=4] {'mp'}, use_global_device_ids=true, to_apply=%region_23.24.clone | all-reduce | flops 2880 | bytes 23040
  680.1 76.6 %psum.14 = f32[1,720]{1,0:T(1,128)S(1)} all-reduce(f32[1,720]{1,0:T(1,128)S(1)} %constant_dynamic-slice_fusion), channel_id=1, replica_groups=mesh['dp'=8,'mp'=4] {'dp'}, use_global_device_ids=true, to_apply=%region_24.25 | all-reduce | flops 720 | bytes 5760 | tf_op jit(solution)/shard_map/psum | solution.py:452
  (219 shorter events, 158.1 us)
Async XLA Ops:
  7.2 83.0 %copy-start = (bf16[320,3,1280]{2,0,1:T(8,128)(2,1)S(1)}, bf16[320,3,1280]{2,0,1:T(8,128)(2,1)}, u32[]{:S(2)}) copy-start(bf16[320,3,1280]{2,0,1:T(8,128)(2,1)} %param.21) | copy-start | bytes 7372804
  7.2 74.6 %all-gather.12.cloned.1.call-start = ((), (), s32[]{:S(2)}) async-start(), calls=%async_computation.10 | async-start | bytes 6656000 | tf_op jit(solution)/shard_map/all_gather | solution.py:336
  16.9 180.9 %all-gather.6.cloned.1.call-start = ((), (), s32[]{:S(2)}) async-start(), calls=%async_computation.4 | async-start | bytes 4096000 | tf_op jit(solution)/shard_map/all_gather | solution.py:313
  17.7 186.3 %all-gather.8.cloned.1.call-start = ((), (), s32[]{:S(2)}) async-start(), calls=%async_computation.5 | async-start | bytes 4096000 | tf_op jit(solution)/shard_map/all_gather | solution.py:314
  18.4 223.4 %all-gather.10.cloned.1.call-start = ((), (), s32[]{:S(2)}) async-start(), calls=%async_computation.6 | async-start | bytes 4096000 | tf_op jit(solution)/shard_map/all_gather | solution.py:315
  19.9 65.4 %copy-start.22 = (s32[2]{0:T(128)}, s32[2]{0:T(128)S(1)}, u32[]{:S(2)}) copy-start(s32[2]{0:T(128)S(1)} %multiply_subtract_fusion.1) | copy-start | bytes 28
  149.1 44.2 %all-to-all-start = ((bf16[4,2048,80]{2,0,1:T(4,128)(2,1)}), bf16[4,2048,80]{2,0,1:T(4,128)(2,1)}, u32[]{:S(2)}, u32[]{:S(2)}) async-start(bf16[4,2048,80]{2,0,1:T(4,128)(2,1)} %copy.44), calls=%async_computation | async-start | bytes 4194304 | tf_op jit(solution)/shard_map/all_to_all | solution.py:366
  153.6 218.5 %reduce-scatter.3.cloned.1.call-start = ((), (), s32[]{:S(2)}) async-start(), calls=%async_computation.7 | async-start | bytes 12288000 | tf_op jit(solution)/shard_map/reduce_scatter | solution.py:400
  265.5 35.8 %all-to-all-start.1 = ((bf16[16,512,80]{1,2,0:T(8,128)(2,1)}), bf16[16,512,80]{1,2,0:T(8,128)(2,1)}, u32[]{:S(2)}, u32[]{:S(2)}) async-start(bf16[16,512,80]{1,2,0:T(8,128)(2,1)} %fusion.26), calls=%async_computation.1 | async-start | bytes 2621440 | tf_op jit(solution)/shard_map/all_to_all | solution.py:392
  269.8 488.1 %all-reduce.7.cloned.1.call-start = ((), (), s32[]{:S(2)}) async-start(), calls=%async_computation.9 | async-start | bytes 9830400 | tf_op jit(solution)/shard_map/psum | solution.py:456
  345.3 10.2 %slice-start = ((s8[5242880]{0:T(1024)(128)(4,1)}), s8[4194304]{0:T(1024)(128)(4,1)S(1)}, s32[]{:S(2)}) async-start(s8[5242880]{0:T(1024)(128)(4,1)} %bitcast.176), calls=%async_computation.11 | async-start | bytes 8388608
  345.9 9.7 %slice-start.1 = ((s8[5242880]{0:T(1024)(128)(4,1)}), s8[1048576]{0:T(1024)(128)(4,1)S(1)}, s32[]{:S(2)}) async-start(s8[5242880]{0:T(1024)(128)(4,1)} %bitcast.176), calls=%async_computation.12 | async-start | bytes 2097152
  376.5 389.2 %reduce-scatter.5.cloned.1.call-start = ((), (), s32[]{:S(2)}) async-start(), calls=%async_computation.8 | async-start | bytes 6553600 | tf_op jit(solution)/shard_map/reduce_scatter | solution.py:433
  389.7 22.2 %copy-start.34 = (u32[32]{0:T(128)S(1)}, u32[32]{0:T(128)}, u32[]{:S(2)}) copy-start(u32[32]{0:T(128)} %constant.234) | copy-start | bytes 388
  389.8 36.4 %copy-start.11 = (bf16[1,4,2048,80]{3,2,1,0:T(8,128)(2,1)S(1)}, bf16[1,4,2048,80]{3,2,1,0:T(8,128)(2,1)}, u32[]{:S(2)}) copy-start(bf16[1,4,2048,80]{3,2,1,0:T(8,128)(2,1)} %get-tuple-element.70) | copy-start | bytes 3932164
  436.7 15.2 %copy-start.5 = (bf16[2,2048,4,80]{1,3,2,0:T(8,128)(2,1)S(1)}, bf16[2,2048,4,80]{1,3,2,0:T(8,128)(2,1)}, u32[]{:S(2)}) copy-start(bf16[2,2048,4,80]{1,3,2,0:T(8,128)(2,1)} %copy.52) | copy-start | bytes 7864324
  436.7 18.7 %copy-start.36 = (f32[512,1280]{1,0:T(8,128)S(1)}, f32[512,1280]{1,0:T(8,128)}, u32[]{:S(2)}) copy-start(f32[512,1280]{1,0:T(8,128)} %copy-done.35) | copy-start | bytes 7864324
  445.4 61.3 %collective-permute-start = (bf16[2,1024,320]{1,2,0:T(8,128)(2,1)}, bf16[2,1024,320]{1,2,0:T(8,128)(2,1)}, u32[]{:S(2)}, u32[]{:S(2)}) collective-permute-start(bf16[2,1024,320]{1,2,0:T(8,128)(2,1)} %get-tuple-element.80), channel_id=1, source_target_pairs={{0,4},{4,8},{8,12},{12,16},{16,20},{20,24},{24,28},{28,0},{1,5},{5... | collective-permute-start | bytes 3932168 | tf_op jit(solution)/shard_map/ppermute | solution.py:357
  445.5 63.7 %collective-permute-start.1 = (bf16[2,1024,320]{1,2,0:T(8,128)(2,1)}, bf16[2,1024,320]{1,2,0:T(8,128)(2,1)}, u32[]{:S(2)}, u32[]{:S(2)}) collective-permute-start(bf16[2,1024,320]{1,2,0:T(8,128)(2,1)} %get-tuple-element.81), channel_id=1, source_target_pairs={{0,8},{4,12},{8,16},{12,20},{16,24},{20,28},{24,0},{28,4},{1,9},{5... | collective-permute-start | bytes 3932168 | tf_op jit(solution)/shard_map/ppermute | solution.py:357
  447.0 172.2 %collective-permute-start.2 = (bf16[2,1024,320]{1,2,0:T(8,128)(2,1)}, bf16[2,1024,320]{1,2,0:T(8,128)(2,1)}, u32[]{:S(2)}, u32[]{:S(2)}) collective-permute-start(bf16[2,1024,320]{1,2,0:T(8,128)(2,1)} %get-tuple-element.82), channel_id=1, source_target_pairs={{0,12},{4,16},{8,20},{12,24},{16,28},{20,0},{24,4},{28,8},{1,13},{... | collective-permute-start | bytes 3932168 | tf_op jit(solution)/shard_map/ppermute | solution.py:357
  449.4 172.2 %collective-permute-start.3 = (bf16[2,1024,320]{1,2,0:T(8,128)(2,1)}, bf16[2,1024,320]{1,2,0:T(8,128)(2,1)}, u32[]{:S(2)}, u32[]{:S(2)}) collective-permute-start(bf16[2,1024,320]{1,2,0:T(8,128)(2,1)} %get-tuple-element.83), channel_id=1, source_target_pairs={{0,16},{4,20},{8,24},{12,28},{16,0},{20,4},{24,8},{28,12},{1,17},{... | collective-permute-start | bytes 3932168 | tf_op jit(solution)/shard_map/ppermute | solution.py:357
  450.8 173.4 %collective-permute-start.4 = (bf16[2,1024,320]{1,2,0:T(8,128)(2,1)}, bf16[2,1024,320]{1,2,0:T(8,128)(2,1)}, u32[]{:S(2)}, u32[]{:S(2)}) collective-permute-start(bf16[2,1024,320]{1,2,0:T(8,128)(2,1)} %get-tuple-element.84), channel_id=1, source_target_pairs={{0,20},{4,24},{8,28},{12,0},{16,4},{20,8},{24,12},{28,16},{1,21},{... | collective-permute-start | bytes 3932168 | tf_op jit(solution)/shard_map/ppermute | solution.py:357
  506.7 120.0 %collective-permute-start.5 = (bf16[2,1024,320]{1,2,0:T(8,128)(2,1)}, bf16[2,1024,320]{1,2,0:T(8,128)(2,1)S(1)}, u32[]{:S(2)}, u32[]{:S(2)}) collective-permute-start(bf16[2,1024,320]{1,2,0:T(8,128)(2,1)} %fusion.35), channel_id=1, source_target_pairs={{0,24},{4,28},{8,0},{12,4},{16,8},{20,12},{24,16},{28,20},{1,25},{... | collective-permute-start | bytes 3932168 | tf_op jit(solution)/shard_map/ppermute | solution.py:357
  509.2 143.5 %collective-permute-start.6 = (bf16[2,1024,320]{1,2,0:T(8,128)(2,1)S(1)}, bf16[2,1024,320]{1,2,0:T(8,128)(2,1)S(1)}, u32[]{:S(2)}, u32[]{:S(2)}) collective-permute-start(bf16[2,1024,320]{1,2,0:T(8,128)(2,1)S(1)} %get-tuple-element.79), channel_id=1, source_target_pairs={{0,28},{4,0},{8,4},{12,8},{16,12},{20,16},{24,20},{28,24},{1,29},{... | collective-permute-start | bytes 3932168 | tf_op jit(solution)/shard_map/ppermute | solution.py:357
  (31 other events, 114.2 us)
Sparse Core Ops, SparseCore 0:
  17.0 64.6 all-gather.11
  83.6 44.9 all-gather.5
  130.5 62.9 all-gather.7
  195.1 46.6 all-gather.9
  259.9 112.1 reduce-scatter.2
  376.6 278.5 all-reduce.6
  658.2 78.6 reduce-scatter.4
where the time goes:
time: 789 us; the launch traced here: 779 us
  waiting for transfers between devices  306 us (39%)
  blocking collectives  92.8 us (12%)
  other arithmetic  88.4 us (11%)
  local copies, waits for them, and re-layouts  79.7 us (10%)
  Pallas kernels  62.5 us (8%)
  matrix products  60.3 us (8%)
  starting transfers between devices  50 us (6%)
  between operations  39.6 us (5%)
    ppermute x7, waiting for transfers between devices, per_device(): lax.ppermute(windows[shift], 'dp', [(r, (r + shift) % groups) for r in ra...  145 us
    psum x1, blocking collectives, per_device(): lax.psum(lax.psum_scatter(small, 'mp', scatter_dimension=0, tiled=True),...  76.6 us
    all_gather x1, waiting for transfers between devices, per_device(): lax.all_gather(jnp.concatenate([tokens, gain_rows]), 'mp', axis=0, tiled=...  60.8 us
    ppermute x7, starting transfers between devices, per_device(): lax.ppermute(windows[shift], 'dp', [(r, (r + shift) % groups) for r in ra...  40.9 us
    all_to_all x1, waiting for transfers between devices, per_device(): lax.all_to_all(att_group, 'mp', split_axis=1, concat_axis=0, tiled=True)  39.5 us
    pallas_call x1, Pallas kernels, attention_backward(): pl.pallas_call(attn_bwd_kernel, grid_spec=pltpu.PrefetchScalarGridSpec(nu...  34.9 us
    pallas_call x1, Pallas kernels, attention_forward(): pl.pallas_call(attn_fwd_kernel, grid_spec=pltpu.PrefetchScalarGridSpec(nu...  27.6 us
    all_gather x1, waiting for transfers between devices, per_device(): lax.all_gather(hidden_out, 'mp', axis=0, tiled=True)  27.4 us
  transfers between devices with their start and end apart: 16, of which 8 were waited for; matrix products, arithmetic and copies ran while one was open for 23% of the time, Pallas kernels for 8%

commit v1 on v0

--- a/solution.py
+++ b/solution.py
@@ -112,6 +112,17 @@
         inside = (rows >= place_start[q]) & (rows < place_start[q] + place_len[q])
         placed = jnp.where(inside, shifted, placed)
     return placed
+
+
+def scatter_sum(partial, axis, count, me):
+    size = partial.shape[0] // count
+    total = lax.dynamic_slice_in_dim(partial, me * size, size, 0).astype(jnp.float32)
+    for shift in range(1, count):
+        piece = lax.dynamic_slice_in_dim(partial, ((me + shift) % count) * size, size, 0)
+        total = total + lax.ppermute(
+            piece, axis, [(r, (r + shift) % count) for r in range(count)]
+        ).astype(jnp.float32)
+    return total
 
 
 def dealt_places(lengths, dealing, series_grp, my_group):
@@ -430,9 +441,7 @@
         * (scale_base / math.sqrt(HD))
         * jax.nn.sigmoid(query_scale)
     )
-    normed_one_grad = lax.psum_scatter(
-        normed_one_part.astype(jnp.bfloat16), "mp", scatter_dimension=0, tiled=True
-    ).astype(jnp.float32)
+    normed_one_grad = scatter_sum(normed_one_part.astype(jnp.bfloat16), "mp", mp_count, my_part)
     scaled_one = gain_first * normed_one_grad
     tokens_grad = (
         first_grad

time: 789 us -> 783 us (level)
  waiting for transfers between devices: 306 us -> 257 us
  blocking collectives: 92.8 us -> 131 us
    ppermute x7, waiting for transfers between devices: 145 us -> 97.4 us  [per_device(): lax.ppermute(windows[shift], 'dp', [(r, (r + shift) % groups) for r in ra...]
    unnamed x1, blocking collectives: 16.1 us -> 55.1 us
    psum x1, waiting for transfers between devices: 0.01 us -> 29.4 us  [per_device(): lax.psum(jnp.concatenate([qkv_part.astype(jnp.bfloat16), shares], axis=1)...]
    all_to_all x1, waiting for transfers between devices: 21 us -> 0.01 us  [per_device(): lax.all_to_all(att_heads_grad, 'mp', split_axis=0, concat_axis=1, tiled=T...]
    reduce_scatter x1, waiting for transfers between devices: 10.1 us -> 0.02 us  [per_device(): lax.psum_scatter(row_terms.astype(jnp.bfloat16), 'mp', scatter_dimension=...]
    ppermute x7, starting transfers between devices: 40.9 us -> 32.5 us  [per_device(): lax.ppermute(windows[shift], 'dp', [(r, (r + shift) % groups) for r in ra...]
    unnamed x87 -> x71, local copies, waits for them, and re-layouts: 24.4 us -> 25 us
  transfers between devices with their start and end apart: 16 -> 18, of which waited for: 8 -> 6; matrix products, arithmetic and copies ran while one was open for 23% -> 23% of each run, Pallas kernels for 8% -> 8%
where the time goes in v1:
time: 783 us; the launch traced here: 773 us
  waiting for transfers between devices  257 us (33%)
  blocking collectives  131 us (17%)
  other arithmetic  91.1 us (12%)
  local copies, waits for them, and re-layouts  83.7 us (11%)
  Pallas kernels  62.9 us (8%)
  matrix products  62.1 us (8%)
  starting transfers between devices  45.9 us (6%)
  between operations  39.5 us (5%)
    ppermute x7, waiting for transfers between devices, per_device(): lax.ppermute(windows[shift], 'dp', [(r, (r + shift) % groups) for r in ra...  97.4 us
    psum x1, blocking collectives, per_device(): lax.psum(lax.psum_scatter(small, 'mp', scatter_dimension=0, tiled=True),...  75.7 us
    all_gather x1, waiting for transfers between devices, per_device(): lax.all_gather(jnp.concatenate([tokens, gain_rows]), 'mp', axis=0, tiled=...  61.3 us
    unnamed x1, blocking collectives  55.1 us
    all_to_all x1, waiting for transfers between devices, per_device(): lax.all_to_all(att_group, 'mp', split_axis=1, concat_axis=0, tiled=True)  39.5 us
    pallas_call x1, Pallas kernels, attention_backward(): pl.pallas_call(attn_bwd_kernel, grid_spec=pltpu.PrefetchScalarGridSpec(nu...  34.9 us
    ppermute x7, starting transfers between devices, per_device(): lax.ppermute(windows[shift], 'dp', [(r, (r + shift) % groups) for r in ra...  32.5 us
    psum x1, waiting for transfers between devices, per_device(): lax.psum(jnp.concatenate([qkv_part.astype(jnp.bfloat16), shares], axis=1)...  29.4 us
  transfers between devices with their start and end apart: 18, of which 6 were waited for; matrix products, arithmetic and copies ran while one was open for 23% of the time, Pallas kernels for 8%

profile of v1, /device:TPU:0, one launch (start us, length us, event | category | flops | bytes accessed | tf_op | source)
XLA Modules:
  0.0 773.1 jit_solution(7106418416108542945)
XLA Ops:
  20.5 61.3 %all-gather.12.cloned.1.call-done = bf16[2080,1280]{1,0:T(8,128)(2,1)} async-done(((bf16[520,1280]{1,0:T(8,128)(2,1)}), bf16[2080,1280]{1,0:T(8,128)(2,1)}) %all-gather.12.cloned.1.call-update) | async-done | bytes 5324816 | tf_op jit(solution)/shard_map/all_gather | solution.py:347
  90.1 8.5 %convolution_bitcast_fusion.1 = f32[3,4,2048,80]{3,2,1,0:T(8,128)S(1)} fusion(bf16[2048,1280,1,1]{1,0,2,3:T(8,128)(2,1)S(1)} %bitcast.180, bf16[4,80,3,1280]{3,1,0,2:T(8,128)(2,1)S(1)} %bitcast.162), kind=kOutput, calls=%fused_computation.21 | convolution fusion | flops 5033164800 | bytes 15564800 | tf_op jit(solution)/shard_map/rd,hecd->chre/dot_general | solution.py:356
  103.5 6.9 fusion.60
  110.4 28.0 %shard_map.186 = (bf16[4,2048,80]{2,1,0:T(8,128)(2,1)S(1)}, f32[4,2048,1]{2,1,0:T(8,128)}) custom-call(s32[16]{0:T(128)S(1)} %get-tuple-element.97.starts_ref, s32[16]{0:T(128)S(1)} %get-tuple-element.96.ends_ref, bf16[4,2048,80]{2,1,0:T(8,128)(2,1)S(1)} %multiply_convert_fusion.q_ref, bf16[4,2048,80]{2,1,0:T(8,128)(2,1)} %bitcast.176, ...), custom_call_target="tpu_custom_call" | custom-call | flops 2684354560 | bytes 5242880 | tf_op jit(solution)/shard_map/pallas_call | solution.py:261
  138.9 10.7 %copy.44 = bf16[4,2048,80]{2,0,1:T(4,128)(2,1)} copy(bf16[4,2048,80]{2,1,0:T(8,128)(2,1)S(1)} %broadcast_select_fusion.1) | data formatting | bytes 2621440 | tf_op jit(solution)/shard_map/jit(_where)/select_n | solution.py:376
  154.3 39.5 %all-to-all-done = bf16[4,2048,80]{2,0,1:T(4,128)(2,1)} async-done(((bf16[4,2048,80]{2,0,1:T(4,128)(2,1)}), bf16[4,2048,80]{2,0,1:T(4,128)(2,1)}, u32[]{:S(2)}, u32[]{:S(2)}) %all-to-all-start) | async-done | bytes 1310752 | tf_op jit(solution)/shard_map/all_to_all | solution.py:377
  198.0 6.2 multiply_reduce_fusion.2
  214.6 27.4 %all-gather.10.cloned.1.call-done = bf16[1280,1280]{1,0:T(8,128)(2,1)} async-done(((bf16[320,1280]{1,0:T(8,128)(2,1)}), bf16[1280,1280]{1,0:T(8,128)(2,1)}) %all-gather.10.cloned.1.call-update) | async-done | bytes 3276816 | tf_op jit(solution)/shard_map/all_gather | solution.py:326
  242.0 5.5 fusion.17
  296.2 5.4 maximum_bitcast_fusion
  301.7 6.0 copy.52
  307.7 9.2 %fusion.36 = (bf16[2,1024,320]{1,2,0:T(8,128)(2,1)}, bf16[2,1024,320]{1,2,0:T(8,128)(2,1)}, bf16[2,1024,320]{1,2,0:T(8,128)(2,1)}, bf16[2,1024,320]{1,2,0:T(8,12...) fusion(s32[]{:T(128)S(6)} %select_n.336, bf16[2,2048,320]{1,2,0:T(8,128)(2,1)} %bitcast.171, ...), kind=kLoop, calls=%fused_computation.92 | loop fusion | flops 3932160 | bytes 10491928 | tf_op jit(solution)/shard_map/jit(_where)/select_n | solution.py:100
  327.0 5.3 slice_bitcast_fusion
  343.5 7.1 fusion.16
  353.9 25.2 %collective-permute-start.9 = (bf16[2,1024,320]{1,2,0:T(8,128)(2,1)S(1)}, bf16[2,1024,320]{1,2,0:T(8,128)(2,1)S(1)}, u32[]{:S(2)}, u32[]{:S(2)}) collective-permute-start(bf16[2,1024,320]{1,2,0:T(8,128)(2,1)S(1)} %copy-done.17), channel_id=1, source_target_pairs={{0,28},{4,0},{8,4},{12,8},{16,12},{20,16},{24,20},{28,24},{1,29},{... | collective-permute-start | bytes 3932168 | tf_op jit(solution)/shard_map/ppermute | solution.py:368
  381.6 80.8 %collective-permute-done.5 = bf16[2,1024,320]{1,2,0:T(8,128)(2,1)} collective-permute-done((bf16[2,1024,320]{1,2,0:T(8,128)(2,1)}, bf16[2,1024,320]{1,2,0:T(8,128)(2,1)}, u32[]{:S(2)}, u32[]{:S(2)}) %collective-permute-start.5) | collective-permute-done | bytes 1310752 | tf_op jit(solution)/shard_map/ppermute | solution.py:368
  471.2 16.5 %collective-permute-done.9 = bf16[2,1024,320]{1,2,0:T(8,128)(2,1)S(1)} collective-permute-done((bf16[2,1024,320]{1,2,0:T(8,128)(2,1)S(1)}, bf16[2,1024,320]{1,2,0:T(8,128)(2,1)S(1)}, u32[]{:S(2)}, u32[]{:S(2)}) %collective-permute-start.9) | collective-permute-done | bytes 1310752 | tf_op jit(solution)/shard_map/ppermute | solution.py:368
  502.2 34.9 %shard_map.187 = (bf16[4,2048,80]{2,1,0:T(8,128)(2,1)S(1)}, bf16[4,2048,80]{2,1,0:T(8,128)(2,1)S(1)}, bf16[4,2048,80]{2,1,0:T(8,128)(2,1)}) custom-call(s32[16]{0:T(128)S(1)} %get-tuple-element.97.starts_ref, s32[16]{0:T(128)S(1)} %get-tuple-element.96.ends_ref, bf16[4,2048,80]{2,1,0:T(8,128)(2,1)} %copy-done.2, bf16[4,2048,80]{2,1,0:T(8,128)(2,1)} %bitcast.177, ...), custom_call_target="tpu_custom_call" | custom-call | flops 6710886400 | bytes 9175040 | tf_op jit(solution)/shard_map/pallas_call | solution.py:288
  540.0 9.6 %convolution_bitcast_fusion = f32[2048,1280]{1,0:T(8,128)} fusion(bf16[4,80,3,1280]{3,1,0,2:T(8,128)(2,1)S(1)} %bitcast.163, bf16[1,4,2048,80]{3,2,1,0:T(8,128)(2,1)S(1)} %get-tuple-element.93, bf16[1,4,2048,80]{3,2,1,0:T(8,128)(2,1)S(1)} %get-tuple-element.92, bf16[1,4,2048,80]{3,2,1,0:T(8,128)(2,1)S(1)} %fusion.25), kind=kOutput, calls=%fused_computation.13 | convolution fusion | flops 5037096960 | bytes 16875520 | tf_op jit(solution)/shard_map/chre,hecd->rd/dot_general | solution.py:432
  549.6 6.9 fusion.10
  556.6 12.6 %fusion.6 = (f32[1280]{0:T(1024)S(1)}, bf16[2048,1280]{1,0:T(8,128)(2,1)}) fusion(f32[2048,1280]{1,0:T(8,128)} %convolution_bitcast_fusion, f32[2048]{0:T(1024)S(1)} %bitcast.185, bf16[4,520,1280]{2,1,0:T(8,128)(2,1)} %bitcast.167), kind=kLoop, calls=%fused_computation.11 | loop fusion | flops 13105920 | bytes 20984832 | tf_op jit(solution)/shard_map/reduce_sum | solution.py:451
  584.2 55.1 %all-reduce.4 = f32[4,720]{1,0:T(4,128)S(1)} all-reduce(f32[4,720]{1,0:T(4,128)S(1)} %maximum_maximum_fusion), channel_id=4, replica_groups=mesh['dp'=8,'mp'=4] {'mp'}, use_global_device_ids=true, to_apply=%region_22.23.clone | all-reduce | flops 2880 | bytes 23040
  640.0 75.7 %psum.14 = f32[1,720]{1,0:T(1,128)S(1)} all-reduce(f32[1,720]{1,0:T(1,128)S(1)} %constant_dynamic-slice_fusion.3), channel_id=1, replica_groups=mesh['dp'=8,'mp'=4] {'dp'}, use_global_device_ids=true, to_apply=%region_23.24 | all-reduce | flops 720 | bytes 5760 | tf_op jit(solution)/shard_map/psum | solution.py:461
  726.5 29.4 %all-reduce.7.cloned.1.call-done = bf16[320,6,1280]{2,0,1:T(8,128)(2,1)} async-done(((bf16[320,6,1280]{2,0,1:T(8,128)(2,1)}), bf16[320,6,1280]{2,0,1:T(8,128)(2,1)}) %all-reduce.7.cloned.1.call-update) | async-done | bytes 4915216 | tf_op jit(solution)/shard_map/psum | solution.py:465
  (208 shorter events, 159.8 us)
Async XLA Ops:
  7.2 83.0 %copy-start = (bf16[320,3,1280]{2,0,1:T(8,128)(2,1)S(1)}, bf16[320,3,1280]{2,0,1:T(8,128)(2,1)}, u32[]{:S(2)}) copy-start(bf16[320,3,1280]{2,0,1:T(8,128)(2,1)} %param.21) | copy-start | bytes 7372804
  7.2 74.6 %all-gather.12.cloned.1.call-start = ((), (), s32[]{:S(2)}) async-start(), calls=%async_computation.8 | async-start | bytes 6656000 | tf_op jit(solution)/shard_map/all_gather | solution.py:347
  16.9 181.1 %all-gather.6.cloned.1.call-start = ((), (), s32[]{:S(2)}) async-start(), calls=%async_computation.3 | async-start | bytes 4096000 | tf_op jit(solution)/shard_map/all_gather | solution.py:324
  17.7 186.5 %all-gather.8.cloned.1.call-start = ((), (), s32[]{:S(2)}) async-start(), calls=%async_computation.4 | async-start | bytes 4096000 | tf_op jit(solution)/shard_map/all_gather | solution.py:325
  18.4 223.6 %all-gather.10.cloned.1.call-start = ((), (), s32[]{:S(2)}) async-start(), calls=%async_computation.5 | async-start | bytes 4096000 | tf_op jit(solution)/shard_map/all_gather | solution.py:326
  149.6 44.1 %all-to-all-start = ((bf16[4,2048,80]{2,0,1:T(4,128)(2,1)}), bf16[4,2048,80]{2,0,1:T(4,128)(2,1)}, u32[]{:S(2)}, u32[]{:S(2)}) async-start(bf16[4,2048,80]{2,0,1:T(4,128)(2,1)} %copy.44), calls=%async_computation | async-start | bytes 4194304 | tf_op jit(solution)/shard_map/all_to_all | solution.py:377
  154.0 402.5 %reduce-scatter.2.cloned.1.call-start = ((), (), s32[]{:S(2)}) async-start(), calls=%async_computation.6 | async-start | bytes 12288000 | tf_op jit(solution)/shard_map/reduce_scatter | solution.py:411
  260.2 21.8 %copy-start.25 = (u32[32]{0:T(128)S(1)}, u32[32]{0:T(128)}, u32[]{:S(2)}) copy-start(u32[32]{0:T(128)} %constant.249) | copy-start | bytes 388
  307.7 15.8 %copy-start.3 = (bf16[2,2048,4,80]{1,3,2,0:T(8,128)(2,1)S(1)}, bf16[2,2048,4,80]{1,3,2,0:T(8,128)(2,1)}, u32[]{:S(2)}) copy-start(bf16[2,2048,4,80]{1,3,2,0:T(8,128)(2,1)} %copy.52) | copy-start | bytes 7864324
  316.9 33.8 %collective-permute-start.3 = (bf16[2,1024,320]{1,2,0:T(8,128)(2,1)}, bf16[2,1024,320]{1,2,0:T(8,128)(2,1)}, u32[]{:S(2)}, u32[]{:S(2)}) collective-permute-start(bf16[2,1024,320]{1,2,0:T(8,128)(2,1)} %get-tuple-element.83), channel_id=1, source_target_pairs={{0,4},{4,8},{8,12},{12,16},{16,20},{20,24},{24,28},{28,0},{1,5},{5... | collective-permute-start | bytes 3932168 | tf_op jit(solution)/shard_map/ppermute | solution.py:368
  316.9 37.0 %collective-permute-start.4 = (bf16[2,1024,320]{1,2,0:T(8,128)(2,1)}, bf16[2,1024,320]{1,2,0:T(8,128)(2,1)}, u32[]{:S(2)}, u32[]{:S(2)}) collective-permute-start(bf16[2,1024,320]{1,2,0:T(8,128)(2,1)} %get-tuple-element.84), channel_id=1, source_target_pairs={{0,8},{4,12},{8,16},{12,20},{16,24},{20,28},{24,0},{28,4},{1,9},{5... | collective-permute-start | bytes 3932168 | tf_op jit(solution)/shard_map/ppermute | solution.py:368
  318.5 143.9 %collective-permute-start.5 = (bf16[2,1024,320]{1,2,0:T(8,128)(2,1)}, bf16[2,1024,320]{1,2,0:T(8,128)(2,1)}, u32[]{:S(2)}, u32[]{:S(2)}) collective-permute-start(bf16[2,1024,320]{1,2,0:T(8,128)(2,1)} %get-tuple-element.85), channel_id=1, source_target_pairs={{0,12},{4,16},{8,20},{12,24},{16,28},{20,0},{24,4},{28,8},{1,13},{... | collective-permute-start | bytes 3932168 | tf_op jit(solution)/shard_map/ppermute | solution.py:368
  321.1 143.8 %collective-permute-start.6 = (bf16[2,1024,320]{1,2,0:T(8,128)(2,1)}, bf16[2,1024,320]{1,2,0:T(8,128)(2,1)}, u32[]{:S(2)}, u32[]{:S(2)}) collective-permute-start(bf16[2,1024,320]{1,2,0:T(8,128)(2,1)} %get-tuple-element.86), channel_id=1, source_target_pairs={{0,16},{4,20},{8,24},{12,28},{16,0},{20,4},{24,8},{28,12},{1,17},{... | collective-permute-start | bytes 3932168 | tf_op jit(solution)/shard_map/ppermute | solution.py:368
  322.2 145.2 %collective-permute-start.7 = (bf16[2,1024,320]{1,2,0:T(8,128)(2,1)}, bf16[2,1024,320]{1,2,0:T(8,128)(2,1)}, u32[]{:S(2)}, u32[]{:S(2)}) collective-permute-start(bf16[2,1024,320]{1,2,0:T(8,128)(2,1)} %get-tuple-element.87), channel_id=1, source_target_pairs={{0,20},{4,24},{8,28},{12,0},{16,4},{20,8},{24,12},{28,16},{1,21},{... | collective-permute-start | bytes 3932168 | tf_op jit(solution)/shard_map/ppermute | solution.py:368
  339.2 156.1 %all-to-all-start.1 = ((bf16[16,512,80]{1,2,0:T(8,128)(2,1)}), bf16[16,512,80]{1,2,0:T(8,128)(2,1)}, u32[]{:S(2)}, u32[]{:S(2)}) async-start(bf16[16,512,80]{1,2,0:T(8,128)(2,1)} %fusion.26), calls=%async_computation.1 | async-start | bytes 2621440 | tf_op jit(solution)/shard_map/all_to_all | solution.py:403
  343.5 412.4 %all-reduce.7.cloned.1.call-start = ((), (), s32[]{:S(2)}) async-start(), calls=%async_computation.7 | async-start | bytes 9830400 | tf_op jit(solution)/shard_map/psum | solution.py:465
  350.7 119.2 %collective-permute-start.8 = (bf16[2,1024,320]{1,2,0:T(8,128)(2,1)}, bf16[2,1024,320]{1,2,0:T(8,128)(2,1)S(1)}, u32[]{:S(2)}, u32[]{:S(2)}) collective-permute-start(bf16[2,1024,320]{1,2,0:T(8,128)(2,1)} %fusion.35), channel_id=1, source_target_pairs={{0,24},{4,28},{8,0},{12,4},{16,8},{20,12},{24,16},{28,20},{1,25},{... | collective-permute-start | bytes 3932168 | tf_op jit(solution)/shard_map/ppermute | solution.py:368
  353.9 133.8 %collective-permute-start.9 = (bf16[2,1024,320]{1,2,0:T(8,128)(2,1)S(1)}, bf16[2,1024,320]{1,2,0:T(8,128)(2,1)S(1)}, u32[]{:S(2)}, u32[]{:S(2)}) collective-permute-start(bf16[2,1024,320]{1,2,0:T(8,128)(2,1)S(1)} %copy-done.17), channel_id=1, source_target_pairs={{0,28},{4,0},{8,4},{12,8},{16,12},{20,16},{24,20},{28,24},{1,29},{... | collective-permute-start | bytes 3932168 | tf_op jit(solution)/shard_map/ppermute | solution.py:368
  539.4 10.1 %slice-start.2 = ((s8[5242880]{0:T(1024)(128)(4,1)}), s8[4194304]{0:T(1024)(128)(4,1)S(1)}, s32[]{:S(2)}) async-start(s8[5242880]{0:T(1024)(128)(4,1)} %bitcast.178), calls=%async_computation.11 | async-start | bytes 8388608
  540.0 9.6 %slice-start.3 = ((s8[5242880]{0:T(1024)(128)(4,1)}), s8[1048576]{0:T(1024)(128)(4,1)S(1)}, s32[]{:S(2)}) async-start(s8[5242880]{0:T(1024)(128)(4,1)} %bitcast.178), calls=%async_computation.12 | async-start | bytes 2097152
  569.2 8.7 %copy-start.13 = (bf16[1280,3,4,80]{0,3,2,1:T(8,128)(2,1)S(1)}, bf16[1280,3,4,80]{0,3,2,1:T(8,128)(2,1)}, u32[]{:S(2)}) copy-start(bf16[1280,3,4,80]{0,3,2,1:T(8,128)(2,1)} %fusion.10) | copy-start | bytes 7372804
  573.5 143.4 %collective-permute-start = (bf16[512,1280]{1,0:T(8,128)(2,1)}, bf16[512,1280]{1,0:T(8,128)(2,1)}, u32[]{:S(2)}, u32[]{:S(2)}) collective-permute-start(bf16[512,1280]{1,0:T(8,128)(2,1)} %get-tuple-element.79), channel_id=1, source_target_pairs={{0,1},{1,2},{2,3},{3,0},{4,5},{5,6},{6,7},{7,4},{8,9},{9,10},{10,1... | collective-permute-start | bytes 3932168 | tf_op jit(solution)/shard_map/ppermute | solution.py:122
  575.0 141.9 %collective-permute-start.2 = (bf16[512,1280]{1,0:T(8,128)(2,1)}, bf16[512,1280]{1,0:T(8,128)(2,1)}, u32[]{:S(2)}, u32[]{:S(2)}) collective-permute-start(bf16[512,1280]{1,0:T(8,128)(2,1)} %get-tuple-element.80), channel_id=1, source_target_pairs={{0,3},{1,0},{2,1},{3,2},{4,7},{5,4},{6,5},{7,6},{8,11},{9,8},{10,9... | collective-permute-start | bytes 3932168 | tf_op jit(solution)/shard_map/ppermute | solution.py:122
  576.4 140.5 %collective-permute-start.1 = (bf16[512,1280]{1,0:T(8,128)(2,1)}, bf16[512,1280]{1,0:T(8,128)(2,1)}, u32[]{:S(2)}, u32[]{:S(2)}) collective-permute-start(bf16[512,1280]{1,0:T(8,128)(2,1)} %get-tuple-element.81), channel_id=1, source_target_pairs={{0,2},{1,3},{2,0},{3,1},{4,6},{5,7},{6,4},{7,5},{8,10},{9,11},{10,... | collective-permute-start | bytes 3932168 | tf_op jit(solution)/shard_map/ppermute | solution.py:122
  (25 other events, 103.7 us)
Sparse Core Ops, SparseCore 0:
  17.0 64.6 all-gather.11
  83.6 44.9 all-gather.5
  130.4 63.3 all-gather.7
  195.6 46.4 all-gather.9
  260.3 112.1 reduce-scatter.1
  580.8 175.1 all-reduce.6

commit v2 on v1

--- a/solution.py
+++ b/solution.py
@@ -123,6 +123,19 @@
             piece, axis, [(r, (r + shift) % count) for r in range(count)]
         ).astype(jnp.float32)
     return total
+
+
+def exchange_rows(piece_for, axis, count, me):
+    received = [piece_for(me)]
+    for shift in range(1, count):
+        received.append(
+            lax.ppermute(
+                piece_for((me + shift) % count), axis, [(r, (r + shift) % count) for r in range(count)]
+            )
+        )
+    stacked = jnp.stack(received)
+    order = (me - jnp.arange(count, dtype=jnp.int32)) % count
+    return jnp.take(stacked, order, axis=0)
 
 
 def dealt_places(lengths, dealing, series_grp, my_group):
@@ -458,7 +471,12 @@
         ],
         axis=1,
     )
-    small = lax.psum(lax.psum_scatter(small, "mp", scatter_dimension=0, tiled=True), "dp")
+    small = jnp.sum(
+        exchange_rows(lambda target: small[target], "mp", mp_count, my_part), axis=0
+    )
+    small = jnp.sum(
+        exchange_rows(lambda target: small, "dp", lax.axis_size("dp"), my_group), axis=0
+    )[None]
     gain_one_grad = small[0, :shard_width]
     gain_two_grad = small[0, shard_width : 2 * shard_width]
     query_scale_grad = small[0, 2 * shard_width :]

time: 783 us -> 794 us (1.014)
  blocking collectives: 131 us -> 0 us
  starting transfers between devices: 45.9 us -> 123 us
  waiting for transfers between devices: 257 us -> 318 us
    ppermute x0 -> x10, starting transfers between devices: none -> 77.4 us  [exchange_rows(): lax.ppermute(piece_for((me + shift) % count), axis, [(r, (r + shift) % co...]
    psum x1 -> x0, blocking collectives: 75.7 us -> none  [per_device(): lax.psum(lax.psum_scatter(small, 'mp', scatter_dimension=0, tiled=True),...]
    unnamed x1 -> x0, blocking collectives: 55.1 us -> none
    ppermute x3, waiting for transfers between devices: 0.01 us -> 42.8 us  [scatter_sum(): lax.ppermute(piece, axis, [(r, (r + shift) % count) for r in range(count)])]
    psum x1, waiting for transfers between devices: 29.4 us -> 47.2 us  [per_device(): lax.psum(jnp.concatenate([qkv_part.astype(jnp.bfloat16), shares], axis=1)...]
    unnamed x71 -> x67, local copies, waits for them, and re-layouts: 25 us -> 23.6 us
  transfers between devices with their start and end apart: 18 -> 28, of which waited for: 6 -> 10; matrix products, arithmetic and copies ran while one was open for 23% -> 23% of each run, Pallas kernels for 8% -> 8%
where the time goes in v2:
time: 794 us; the launch traced here: 784 us
  waiting for transfers between devices  318 us (40%)
  starting transfers between devices  123 us (15%)
  other arithmetic  93 us (12%)
  local copies, waits for them, and re-layouts  84.6 us (11%)
  Pallas kernels  62.9 us (8%)
  matrix products  61.7 us (8%)
  between operations  39.9 us (5%)
    ppermute x7, waiting for transfers between devices, per_device(): lax.ppermute(windows[shift], 'dp', [(r, (r + shift) % groups) for r in ra...  97.4 us
    ppermute x10, starting transfers between devices, exchange_rows(): lax.ppermute(piece_for((me + shift) % count), axis, [(r, (r + shift) % co...  77.4 us
    all_gather x1, waiting for transfers between devices, per_device(): lax.all_gather(jnp.concatenate([tokens, gain_rows]), 'mp', axis=0, tiled=...  61 us
    psum x1, waiting for transfers between devices, per_device(): lax.psum(jnp.concatenate([qkv_part.astype(jnp.bfloat16), shares], axis=1)...  47.2 us
    ppermute x3, waiting for transfers between devices, scatter_sum(): lax.ppermute(piece, axis, [(r, (r + shift) % count) for r in range(count)])  42.8 us
    all_to_all x1, waiting for transfers between devices, per_device(): lax.all_to_all(att_group, 'mp', split_axis=1, concat_axis=0, tiled=True)  39.5 us
    pallas_call x1, Pallas kernels, attention_backward(): pl.pallas_call(attn_bwd_kernel, grid_spec=pltpu.PrefetchScalarGridSpec(nu...  34.9 us
    ppermute x7, starting transfers between devices, per_device(): lax.ppermute(windows[shift], 'dp', [(r, (r + shift) % groups) for r in ra...  33.4 us
  transfers between devices with their start and end apart: 28, of which 10 were waited for; matrix products, arithmetic and copies ran while one was open for 23% of the time, Pallas kernels for 8%

profile of v2, /device:TPU:0, one launch (start us, length us, event | category | flops | bytes accessed | tf_op | source)
XLA Modules:
  0.0 783.7 jit_solution(15605946008859881189)
XLA Ops:
  20.8 61.0 %all-gather.12.cloned.1.call-done = bf16[2080,1280]{1,0:T(8,128)(2,1)} async-done(((bf16[520,1280]{1,0:T(8,128)(2,1)}), bf16[2080,1280]{1,0:T(8,128)(2,1)}) %all-gather.12.cloned.1.call-update) | async-done | bytes 5324816 | tf_op jit(solution)/shard_map/all_gather | solution.py:360
  90.1 8.5 %convolution_bitcast_fusion.1 = f32[3,4,2048,80]{3,2,1,0:T(8,128)S(1)} fusion(bf16[2048,1280,1,1]{1,0,2,3:T(8,128)(2,1)S(1)} %bitcast.183, bf16[4,80,3,1280]{3,1,0,2:T(8,128)(2,1)S(1)} %bitcast.165), kind=kOutput, calls=%fused_computation.23 | convolution fusion | flops 5033164800 | bytes 15564800 | tf_op jit(solution)/shard_map/rd,hecd->chre/dot_general | solution.py:369
  103.5 6.9 fusion.69
  110.4 28.0 %shard_map.186 = (bf16[4,2048,80]{2,1,0:T(8,128)(2,1)S(1)}, f32[4,2048,1]{2,1,0:T(8,128)}) custom-call(s32[16]{0:T(128)S(1)} %get-tuple-element.101.starts_ref, s32[16]{0:T(128)S(1)} %get-tuple-element.100.ends_ref, bf16[4,2048,80]{2,1,0:T(8,128)(2,1)S(1)} %multiply_convert_fusion.q_ref, bf16[4,2048,80]{2,1,0:T(8,128)(2,1)} %bitcast.179, ...), custom_call_target="tpu_custom_call" | custom-call | flops 2684354560 | bytes 5242880 | tf_op jit(solution)/shard_map/pallas_call | solution.py:274
  138.9 10.7 %copy.44 = bf16[4,2048,80]{2,0,1:T(4,128)(2,1)} copy(bf16[4,2048,80]{2,1,0:T(8,128)(2,1)S(1)} %broadcast_select_fusion.1) | data formatting | bytes 2621440 | tf_op jit(solution)/shard_map/jit(_where)/select_n | solution.py:389
  154.3 39.5 %all-to-all-done = bf16[4,2048,80]{2,0,1:T(4,128)(2,1)} async-done(((bf16[4,2048,80]{2,0,1:T(4,128)(2,1)}), bf16[4,2048,80]{2,0,1:T(4,128)(2,1)}, u32[]{:S(2)}, u32[]{:S(2)}) %all-to-all-start) | async-done | bytes 1310752 | tf_op jit(solution)/shard_map/all_to_all | solution.py:390
  198.0 6.2 multiply_reduce_fusion.2
  214.7 27.4 %all-gather.10.cloned.1.call-done = bf16[1280,1280]{1,0:T(8,128)(2,1)} async-done(((bf16[320,1280]{1,0:T(8,128)(2,1)}), bf16[1280,1280]{1,0:T(8,128)(2,1)}) %all-gather.10.cloned.1.call-update) | async-done | bytes 3276816 | tf_op jit(solution)/shard_map/all_gather | solution.py:339
  300.9 6.0 copy.52
  307.0 9.2 %fusion.36 = (bf16[2,1024,320]{1,2,0:T(8,128)(2,1)}, bf16[2,1024,320]{1,2,0:T(8,128)(2,1)}, bf16[2,1024,320]{1,2,0:T(8,128)(2,1)}, bf16[2,1024,320]{1,2,0:T(8,12...) fusion(s32[]{:T(128)S(6)} %select_n.428, bf16[2,2048,320]{1,2,0:T(8,128)(2,1)} %bitcast.174, ...), kind=kLoop, calls=%fused_computation.94 | loop fusion | flops 3932160 | bytes 10491928 | tf_op jit(solution)/shard_map/jit(_where)/select_n | solution.py:100
  342.3 6.8 fusion.16
  353.9 24.6 %collective-permute-start.9 = (bf16[2,1024,320]{1,2,0:T(8,128)(2,1)S(1)}, bf16[2,1024,320]{1,2,0:T(8,128)(2,1)S(1)}, u32[]{:S(2)}, u32[]{:S(2)}) collective-permute-start(bf16[2,1024,320]{1,2,0:T(8,128)(2,1)S(1)} %copy-done.17), channel_id=1, source_target_pairs={{0,28},{4,0},{8,4},{12,8},{16,12},{20,16},{24,20},{28,24},{1,29},{... | collective-permute-start | bytes 3932168 | tf_op jit(solution)/shard_map/ppermute | solution.py:381
  380.9 80.8 %collective-permute-done.5 = bf16[2,1024,320]{1,2,0:T(8,128)(2,1)} collective-permute-done((bf16[2,1024,320]{1,2,0:T(8,128)(2,1)}, bf16[2,1024,320]{1,2,0:T(8,128)(2,1)}, u32[]{:S(2)}, u32[]{:S(2)}) %collective-permute-start.5) | collective-permute-done | bytes 1310752 | tf_op jit(solution)/shard_map/ppermute | solution.py:381
  470.4 16.7 %collective-permute-done.9 = bf16[2,1024,320]{1,2,0:T(8,128)(2,1)S(1)} collective-permute-done((bf16[2,1024,320]{1,2,0:T(8,128)(2,1)S(1)}, bf16[2,1024,320]{1,2,0:T(8,128)(2,1)S(1)}, u32[]{:S(2)}, u32[]{:S(2)}) %collective-permute-start.9) | collective-permute-done | bytes 1310752 | tf_op jit(solution)/shard_map/ppermute | solution.py:381
  495.1 34.9 %shard_map.187 = (bf16[4,2048,80]{2,1,0:T(8,128)(2,1)S(1)}, bf16[4,2048,80]{2,1,0:T(8,128)(2,1)S(1)}, bf16[4,2048,80]{2,1,0:T(8,128)(2,1)}) custom-call(s32[16]{0:T(128)S(1)} %get-tuple-element.101.starts_ref, s32[16]{0:T(128)S(1)} %get-tuple-element.100.ends_ref, bf16[4,2048,80]{2,1,0:T(8,128)(2,1)} %copy-done.2, bf16[4,2048,80]{2,1,0:T(8,128)(2,1)} %bitcast.180, ...), custom_call_target="tpu_custom_call" | custom-call | flops 6710886400 | bytes 9175040 | tf_op jit(solution)/shard_map/pallas_call | solution.py:301
  532.9 9.6 %convolution_bitcast_fusion = f32[2048,1280]{1,0:T(8,128)} fusion(bf16[4,80,3,1280]{3,1,0,2:T(8,128)(2,1)S(1)} %bitcast.166, bf16[1,4,2048,80]{3,2,1,0:T(8,128)(2,1)S(1)} %get-tuple-element.97, bf16[1,4,2048,80]{3,2,1,0:T(8,128)(2,1)S(1)} %get-tuple-element.96, bf16[1,4,2048,80]{3,2,1,0:T(8,128)(2,1)S(1)} %fusion.25), kind=kOutput, calls=%fused_computation.15 | convolution fusion | flops 5037096960 | bytes 16875520 | tf_op jit(solution)/shard_map/chre,hecd->rd/dot_general | solution.py:445
  542.4 6.8 fusion.10
  552.8 12.8 %fusion.6 = (f32[1280]{0:T(1024)S(1)}, bf16[2048,1280]{1,0:T(8,128)(2,1)}) fusion(f32[2048,1280]{1,0:T(8,128)} %convolution_bitcast_fusion, f32[2048]{0:T(1024)S(1)} %bitcast.188, bf16[4,520,1280]{2,1,0:T(8,128)(2,1)} %bitcast.170), kind=kLoop, calls=%fused_computation.13 | loop fusion | flops 13105920 | bytes 20984832 | tf_op jit(solution)/shard_map/reduce_sum | solution.py:464
  574.4 62.9 %collective-permute-start.19 = (f32[720]{0:T(1024)S(1)}, f32[720]{0:T(1024)S(1)}, u32[]{:S(2)}, u32[]{:S(2)}) collective-permute-start(f32[720]{0:T(1024)S(1)} %select_reduce_fusion.3), channel_id=1, source_target_pairs={{0,28},{4,0},{8,4},{12,8},{16,12},{20,16},{24,20},{28,24},{1,29},{... | collective-permute-start | bytes 8648 | tf_op jit(solution)/shard_map/ppermute | solution.py:132
  637.4 7.2 collective-permute-start.17
  658.9 6.0 fusion.22
  667.0 14.0 %collective-permute-done = bf16[512,1280]{1,0:T(8,128)(2,1)} collective-permute-done((bf16[512,1280]{1,0:T(8,128)(2,1)}, bf16[512,1280]{1,0:T(8,128)(2,1)}, u32[]{:S(2)}, u32[]{:S(2)}) %collective-permute-start) | collective-permute-done | bytes 1310752 | tf_op jit(solution)/shard_map/ppermute | solution.py:122
  681.0 27.2 %collective-permute-done.2 = bf16[512,1280]{1,0:T(8,128)(2,1)} collective-permute-done((bf16[512,1280]{1,0:T(8,128)(2,1)}, bf16[512,1280]{1,0:T(8,128)(2,1)}, u32[]{:S(2)}, u32[]{:S(2)}) %collective-permute-start.2) | collective-permute-done | bytes 1310752 | tf_op jit(solution)/shard_map/ppermute | solution.py:122
  719.2 47.2 %all-reduce.6.cloned.1.call-done = bf16[320,6,1280]{2,0,1:T(8,128)(2,1)} async-done(((bf16[320,6,1280]{2,0,1:T(8,128)(2,1)}), bf16[320,6,1280]{2,0,1:T(8,128)(2,1)}) %all-reduce.6.cloned.1.call-update) | async-done | bytes 4915216 | tf_op jit(solution)/shard_map/psum | solution.py:483
  (246 shorter events, 182.9 us)
Async XLA Ops:
  7.2 74.6 %all-gather.12.cloned.1.call-start = ((), (), s32[]{:S(2)}) async-start(), calls=%async_computation.8 | async-start | bytes 6656000 | tf_op jit(solution)/shard_map/all_gather | solution.py:360
  16.9 181.1 %all-gather.6.cloned.1.call-start = ((), (), s32[]{:S(2)}) async-start(), calls=%async_computation.3 | async-start | bytes 4096000 | tf_op jit(solution)/shard_map/all_gather | solution.py:337
  17.7 186.5 %all-gather.8.cloned.1.call-start = ((), (), s32[]{:S(2)}) async-start(), calls=%async_computation.4 | async-start | bytes 4096000 | tf_op jit(solution)/shard_map/all_gather | solution.py:338
  18.4 223.6 %all-gather.10.cloned.1.call-start = ((), (), s32[]{:S(2)}) async-start(), calls=%async_computation.5 | async-start | bytes 4096000 | tf_op jit(solution)/shard_map/all_gather | solution.py:339
  149.6 44.1 %all-to-all-start = ((bf16[4,2048,80]{2,0,1:T(4,128)(2,1)}), bf16[4,2048,80]{2,0,1:T(4,128)(2,1)}, u32[]{:S(2)}, u32[]{:S(2)}) async-start(bf16[4,2048,80]{2,0,1:T(4,128)(2,1)} %copy.44), calls=%async_computation | async-start | bytes 4194304 | tf_op jit(solution)/shard_map/all_to_all | solution.py:390
  154.1 395.1 %reduce-scatter.2.cloned.1.call-start = ((), (), s32[]{:S(2)}) async-start(), calls=%async_computation.6 | async-start | bytes 12288000 | tf_op jit(solution)/shard_map/reduce_scatter | solution.py:424
  316.2 33.0 %collective-permute-start.3 = (bf16[2,1024,320]{1,2,0:T(8,128)(2,1)}, bf16[2,1024,320]{1,2,0:T(8,128)(2,1)}, u32[]{:S(2)}, u32[]{:S(2)}) collective-permute-start(bf16[2,1024,320]{1,2,0:T(8,128)(2,1)} %get-tuple-element.86), channel_id=1, source_target_pairs={{0,4},{4,8},{8,12},{12,16},{16,20},{20,24},{24,28},{28,0},{1,5},{5... | collective-permute-start | bytes 3932168 | tf_op jit(solution)/shard_map/ppermute | solution.py:381
  316.2 37.6 %collective-permute-start.4 = (bf16[2,1024,320]{1,2,0:T(8,128)(2,1)}, bf16[2,1024,320]{1,2,0:T(8,128)(2,1)}, u32[]{:S(2)}, u32[]{:S(2)}) collective-permute-start(bf16[2,1024,320]{1,2,0:T(8,128)(2,1)} %get-tuple-element.87), channel_id=1, source_target_pairs={{0,8},{4,12},{8,16},{12,20},{16,24},{20,28},{24,0},{28,4},{1,9},{5... | collective-permute-start | bytes 3932168 | tf_op jit(solution)/shard_map/ppermute | solution.py:381
  317.8 143.9 %collective-permute-start.5 = (bf16[2,1024,320]{1,2,0:T(8,128)(2,1)}, bf16[2,1024,320]{1,2,0:T(8,128)(2,1)}, u32[]{:S(2)}, u32[]{:S(2)}) collective-permute-start(bf16[2,1024,320]{1,2,0:T(8,128)(2,1)} %get-tuple-element.88), channel_id=1, source_target_pairs={{0,12},{4,16},{8,20},{12,24},{16,28},{20,0},{24,4},{28,8},{1,13},{... | collective-permute-start | bytes 3932168 | tf_op jit(solution)/shard_map/ppermute | solution.py:381
  320.4 143.8 %collective-permute-start.6 = (bf16[2,1024,320]{1,2,0:T(8,128)(2,1)}, bf16[2,1024,320]{1,2,0:T(8,128)(2,1)}, u32[]{:S(2)}, u32[]{:S(2)}) collective-permute-start(bf16[2,1024,320]{1,2,0:T(8,128)(2,1)} %get-tuple-element.89), channel_id=1, source_target_pairs={{0,16},{4,20},{8,24},{12,28},{16,0},{20,4},{24,8},{28,12},{1,17},{... | collective-permute-start | bytes 3932168 | tf_op jit(solution)/shard_map/ppermute | solution.py:381
  321.6 145.2 %collective-permute-start.7 = (bf16[2,1024,320]{1,2,0:T(8,128)(2,1)}, bf16[2,1024,320]{1,2,0:T(8,128)(2,1)}, u32[]{:S(2)}, u32[]{:S(2)}) collective-permute-start(bf16[2,1024,320]{1,2,0:T(8,128)(2,1)} %get-tuple-element.90), channel_id=1, source_target_pairs={{0,20},{4,24},{8,28},{12,0},{16,4},{20,8},{24,12},{28,16},{1,21},{... | collective-permute-start | bytes 3932168 | tf_op jit(solution)/shard_map/ppermute | solution.py:381
  337.9 150.3 %all-to-all-start.1 = ((bf16[16,512,80]{1,2,0:T(8,128)(2,1)}), bf16[16,512,80]{1,2,0:T(8,128)(2,1)}, u32[]{:S(2)}, u32[]{:S(2)}) async-start(bf16[16,512,80]{1,2,0:T(8,128)(2,1)} %fusion.26), calls=%async_computation.1 | async-start | bytes 2621440 | tf_op jit(solution)/shard_map/all_to_all | solution.py:416
  342.2 424.2 %all-reduce.6.cloned.1.call-start = ((), (), s32[]{:S(2)}) async-start(), calls=%async_computation.7 | async-start | bytes 9830400 | tf_op jit(solution)/shard_map/psum | solution.py:483
  349.2 120.0 %collective-permute-start.8 = (bf16[2,1024,320]{1,2,0:T(8,128)(2,1)}, bf16[2,1024,320]{1,2,0:T(8,128)(2,1)S(1)}, u32[]{:S(2)}, u32[]{:S(2)}) collective-permute-start(bf16[2,1024,320]{1,2,0:T(8,128)(2,1)} %fusion.35), channel_id=1, source_target_pairs={{0,24},{4,28},{8,0},{12,4},{16,8},{20,12},{24,16},{28,20},{1,25},{... | collective-permute-start | bytes 3932168 | tf_op jit(solution)/shard_map/ppermute | solution.py:381
  353.9 133.1 %collective-permute-start.9 = (bf16[2,1024,320]{1,2,0:T(8,128)(2,1)S(1)}, bf16[2,1024,320]{1,2,0:T(8,128)(2,1)S(1)}, u32[]{:S(2)}, u32[]{:S(2)}) collective-permute-start(bf16[2,1024,320]{1,2,0:T(8,128)(2,1)S(1)} %copy-done.17), channel_id=1, source_target_pairs={{0,28},{4,0},{8,4},{12,8},{16,12},{20,16},{24,20},{28,24},{1,29},{... | collective-permute-start | bytes 3932168 | tf_op jit(solution)/shard_map/ppermute | solution.py:381
  565.9 7.8 collective-permute-start.10
  567.4 6.3 collective-permute-start.12
  574.4 77.4 %collective-permute-start.19 = (f32[720]{0:T(1024)S(1)}, f32[720]{0:T(1024)S(1)}, u32[]{:S(2)}, u32[]{:S(2)}) collective-permute-start(f32[720]{0:T(1024)S(1)} %select_reduce_fusion.3), channel_id=1, source_target_pairs={{0,28},{4,0},{8,4},{12,8},{16,12},{20,16},{24,20},{28,24},{1,29},{... | collective-permute-start | bytes 8648 | tf_op jit(solution)/shard_map/ppermute | solution.py:132
  637.4 15.0 %collective-permute-start.18 = (f32[720]{0:T(1024)S(1)}, f32[720]{0:T(1024)S(1)}, u32[]{:S(2)}, u32[]{:S(2)}) collective-permute-start(f32[720]{0:T(1024)S(1)} %select_reduce_fusion.3), channel_id=1, source_target_pairs={{0,24},{4,28},{8,0},{12,4},{16,8},{20,12},{24,16},{28,20},{1,25},{... | collective-permute-start | bytes 8648 | tf_op jit(solution)/shard_map/ppermute | solution.py:132
  637.4 15.3 %collective-permute-start.17 = (f32[720]{0:T(1024)S(1)}, f32[720]{0:T(1024)S(1)}, u32[]{:S(2)}, u32[]{:S(2)}) collective-permute-start(f32[720]{0:T(1024)S(1)} %select_reduce_fusion.3), channel_id=1, source_target_pairs={{0,20},{4,24},{8,28},{12,0},{16,4},{20,8},{24,12},{28,16},{1,21},{... | collective-permute-start | bytes 8648 | tf_op jit(solution)/shard_map/ppermute | solution.py:132
  648.9 32.1 %collective-permute-start = (bf16[512,1280]{1,0:T(8,128)(2,1)}, bf16[512,1280]{1,0:T(8,128)(2,1)}, u32[]{:S(2)}, u32[]{:S(2)}) collective-permute-start(bf16[512,1280]{1,0:T(8,128)(2,1)} %get-tuple-element.82), channel_id=1, source_target_pairs={{0,1},{1,2},{2,3},{3,0},{4,5},{5,6},{6,7},{7,4},{8,9},{9,10},{10,1... | collective-permute-start | bytes 3932168 | tf_op jit(solution)/shard_map/ppermute | solution.py:122
  648.9 59.3 %collective-permute-start.2 = (bf16[512,1280]{1,0:T(8,128)(2,1)}, bf16[512,1280]{1,0:T(8,128)(2,1)}, u32[]{:S(2)}, u32[]{:S(2)}) collective-permute-start(bf16[512,1280]{1,0:T(8,128)(2,1)} %get-tuple-element.83), channel_id=1, source_target_pairs={{0,3},{1,0},{2,1},{3,2},{4,7},{5,4},{6,5},{7,6},{8,11},{9,8},{10,9... | collective-permute-start | bytes 3932168 | tf_op jit(solution)/shard_map/ppermute | solution.py:122
  651.8 58.0 %collective-permute-start.1 = (bf16[512,1280]{1,0:T(8,128)(2,1)}, bf16[512,1280]{1,0:T(8,128)(2,1)}, u32[]{:S(2)}, u32[]{:S(2)}) collective-permute-start(bf16[512,1280]{1,0:T(8,128)(2,1)} %get-tuple-element.84), channel_id=1, source_target_pairs={{0,2},{1,3},{2,0},{3,1},{4,6},{5,7},{6,4},{7,5},{8,10},{9,11},{10,... | collective-permute-start | bytes 3932168 | tf_op jit(solution)/shard_map/ppermute | solution.py:122
  657.0 8.1 %collective-permute-start.14 = (f32[720]{0:T(1024)S(1)}, f32[720]{0:T(1024)S(1)}, u32[]{:S(2)}, u32[]{:S(2)}) collective-permute-start(f32[720]{0:T(1024)S(1)} %select_reduce_fusion.3), channel_id=1, source_target_pairs={{0,8},{4,12},{8,16},{12,20},{16,24},{20,28},{24,0},{28,4},{1,9},{5... | collective-permute-start | bytes 8648 | tf_op jit(solution)/shard_map/ppermute | solution.py:132
  (34 other events, 347.6 us)
Sparse Core Ops, SparseCore 0:
  17.0 64.6 all-gather.11
  83.6 44.9 all-gather.5
  130.4 63.3 all-gather.7
  195.6 46.4 all-gather.9
  260.3 112.1 reduce-scatter.1
  656.1 110.2 all-reduce.5
